TPU v7x, 128 devices: a whole 4x4x4 slice. The times are simulated.
128 devices in a mesh: ctx: 16 (over y, x), grp: 8 (over z, core).
Axes of the slice: x: 4, y: 4, z: 4, core: 2. Of those that a mesh axis runs over, the one named last changes fastest.
Arguments:
- residual: bfloat16 [8, 2048, 2880], P('grp', 'ctx'), may hold values from -3 to 3
- queries: bfloat16 [8, 2048, 2048], P('grp', 'ctx'), may hold values from -8 to 8
- stretch_kv: bfloat16 [8, 2048, 1024], P('grp', 'ctx'), may hold values from -8 to 8
- cache_kv: bfloat16 [8, 4096, 1024], P('grp', 'ctx'), may hold values from -6 to 6
- doc_lengths: int32 [8, 8], P('grp'), may hold values from 1 to 3072, 6144 in all within a row
- sinks: float32 [32], replicated, may hold values from 2 to 6
- out_proj: bfloat16 [2048, 2880], P('ctx'), may hold values from -0.75 to 0.75
- norm_gain: float32 [2880], replicated, may hold values from 0.1 to 1.9
- router: bfloat16 [2880, 64], replicated, may hold values from -0.109375 to 0.109375
- expert_ids: int32 [8, 2048, 4], P('grp', 'ctx'), may hold values from 0 to 63, all different within a row; in each aligned block of 128 rows (0 to 127, 128 to 255, ..., all dimensions but the last counted through in order) at most 10 rows name the same one
- expert_in: bfloat16 [128, 2880, 1536], P(('ctx', 'grp')), may hold values from -0.109375 to 0.109375
- expert_out: bfloat16 [128, 768, 2880], P(('ctx', 'grp')), may hold values from -0.15625 to 0.15625
Outputs:
- resid_mid: bfloat16 [8, 2048, 2880], P('grp', 'ctx')
- layer_out: bfloat16 [8, 2048, 2880], P('grp', 'ctx')
Inputs may be any that keep to these rules, and one draw needn't show every extreme that they name: `expert_ids`: in the rows of one device (aligned blocks of 128 tokens, sequence after sequence), each expert is named by at most 10 rows, and in some blocks one expert by exactly 10; a token's 4 experts differ. `doc_lengths`: A sequence's 8 lengths sum to 6144; the longest is exactly 3072.
All inputs are finite; a program needn't handle non-finite values.
Results may differ from a plain program's by a relative error of at most 0.015.
Values may be sent and summed in bfloat16 or wider, within the bound.
No kernel may reach another device: no remote copies, remote signals or barrier semaphores. Data moves between devices by JAX's collectives and lax.ppermute only.
A program may use at most 128 MiB of HBM per device.

v0:
```python
import math

import jax
import jax.numpy as jnp
from jax import lax
from jax.sharding import PartitionSpec as P

HEADS = 32
KVH = 8
HD = 64


def doc_index(positions, lengths):
    ends = jnp.cumsum(lengths)
    return jnp.sum((positions[:, None] >= ends[None, :]).astype(jnp.int32), axis=1)


def gated_act(pre, half_width):
    gate = pre[:, :half_width]
    upper = pre[:, half_width:]
    return ((upper + 1.0) * gate * jax.nn.sigmoid(1.702 * gate)).astype(jnp.bfloat16)


def body(
    residual,
    queries,
    stretch_kv,
    cache_kv,
    doc_lengths,
    sinks,
    out_proj,
    norm_gain,
    router,
    expert_ids,
    expert_in,
    expert_out,
):
    tokens = residual.shape[1]
    width = residual.shape[2]
    cache_rows = cache_kv.shape[1]
    kv_cols = stretch_kv.shape[2] // 2
    groups = HEADS // KVH
    ctx_count = lax.axis_size("ctx")
    ctx_here = lax.axis_index("ctx")
    stretch_base = cache_rows * ctx_count
    span = cache_rows + tokens
    query_pos = stretch_base + ctx_here * tokens + jnp.arange(tokens, dtype=jnp.int32)
    lengths = doc_lengths[0]
    query_doc = doc_index(query_pos, lengths)
    query_heads = queries[0].reshape(tokens, KVH, groups, HD)
    sink_grid = sinks.reshape(KVH, groups)
    local_kv = jnp.concatenate([cache_kv[0], stretch_kv[0]], axis=0)
    scale = 1.0 / math.sqrt(HD)

    def key_block(carry, keys_values, first):
        count = keys_values.shape[0]
        rows = first + jnp.arange(count, dtype=jnp.int32)
        source = rows // span
        offset = rows % span
        key_pos = jnp.where(
            offset < cache_rows,
            source * cache_rows + offset,
            stretch_base + source * tokens + offset - cache_rows,
        )
        key_doc = doc_index(key_pos, lengths)
        allowed = (key_pos[None, :] <= query_pos[:, None]) & (
            key_doc[None, :] == query_doc[:, None]
        )
        keys = keys_values[:, :kv_cols].reshape(count, KVH, HD)
        values = keys_values[:, kv_cols:].reshape(count, KVH, HD)
        top, total, numer = carry
        scores = (
            jnp.einsum("qkgd,skd->kgqs", query_heads, keys, preferred_element_type=jnp.float32)
            * scale
        )
        masked = jnp.where(allowed[None, None], scores, -jnp.inf)
        new_top = jnp.maximum(top, jnp.max(masked, axis=-1))
        weights = jnp.where(allowed[None, None], jnp.exp(scores - new_top[..., None]), 0.0)
        shrink = jnp.exp(top - new_top)
        total = total * shrink + jnp.sum(weights, axis=-1)
        numer = numer * shrink[..., None] + jnp.einsum(
            "kgqs,skd->kgqd",
            weights.astype(jnp.bfloat16),
            values,
            preferred_element_type=jnp.float32,
        )
        return (new_top, total, numer)

    start_top = jnp.broadcast_to(sink_grid[:, :, None], (KVH, groups, tokens))
    start_total = jnp.zeros((KVH, groups, tokens), jnp.float32)
    start_numer = jnp.zeros((KVH, groups, tokens, HD), jnp.float32)
    piece = lax.all_gather(local_kv, "ctx", axis=0, tiled=True)
    count = piece.shape[0]
    step_rows = math.gcd(count, 1024)

    def advance(index, state):
        first = index * step_rows
        part = lax.dynamic_slice_in_dim(piece, first, step_rows, 0)
        return key_block(state, part, first)

    top, total, numer = lax.fori_loop(
        0, count // step_rows, advance, (start_top, start_total, start_numer)
    )
    denom = total + jnp.exp(sink_grid[:, :, None] - top)
    attended = (
        jnp.transpose(numer / denom[..., None], (2, 0, 1, 3))
        .reshape(tokens, HEADS * HD)
        .astype(jnp.bfloat16)
    )
    projected = jnp.dot(
        attended,
        lax.all_gather(out_proj, "ctx", axis=0, tiled=True),
        preferred_element_type=jnp.float32,
    )
    mid = (residual[0].astype(jnp.float32) + projected).astype(jnp.bfloat16)
    mid_float = mid.astype(jnp.float32)
    normed = (
        mid_float
        * lax.rsqrt(jnp.mean(mid_float * mid_float, axis=-1, keepdims=True) + 1e-05)
        * norm_gain
    ).astype(jnp.bfloat16)
    logits = jnp.dot(normed, router, preferred_element_type=jnp.float32)
    experts = router.shape[1]
    chosen_ids = expert_ids[0]
    topk = chosen_ids.shape[1]
    picks = chosen_ids[:, :, None] == jnp.arange(experts, dtype=jnp.int32)[None, None, :]
    chosen = jnp.sum(jnp.where(picks, logits[:, None, :], 0.0), axis=-1)
    raised = jnp.exp(chosen)
    route_weights = raised / jnp.sum(raised, axis=-1, keepdims=True)
    capacity = 2 * ((5 * tokens * topk + 8 * experts - 1) // (8 * experts))
    flat_ids = chosen_ids.reshape(-1)
    pairs = flat_ids.shape[0]
    onehot = (flat_ids[:, None] == jnp.arange(experts, dtype=jnp.int32)[None, :]).astype(jnp.int32)
    slots = jnp.sum(onehot * (jnp.cumsum(onehot, axis=0) - 1), axis=1)
    dest = flat_ids * capacity + slots
    source_rows = jnp.arange(pairs, dtype=jnp.int32) // topk
    packed = jnp.zeros((experts * capacity, width), jnp.bfloat16).at[dest].set(normed[source_rows])
    packed = packed.reshape(experts, capacity, width)
    in_weights = expert_in[0]
    out_weights = expert_out[0]
    half_width = out_weights.shape[0]
    doubled = jnp.broadcast_to(packed[:, None], (experts, 2, capacity, width)).reshape(
        2 * experts, capacity, width
    )
    received = lax.all_to_all(doubled, ("ctx", "grp"), split_axis=0, concat_axis=0, tiled=True)
    flat_rows = received.reshape(-1, width)
    pre = jnp.dot(flat_rows, in_weights, preferred_element_type=jnp.float32)
    hidden = gated_act(pre, half_width)
    partial_out = jnp.dot(hidden, out_weights, preferred_element_type=jnp.float32).astype(
        jnp.bfloat16
    )
    partial_out = partial_out.reshape(received.shape)
    returned = lax.all_to_all(partial_out, ("ctx", "grp"), split_axis=0, concat_axis=0, tiled=True)
    pair_total = jnp.sum(returned.reshape(experts, 2, capacity, width).astype(jnp.float32), axis=1)
    expert_rows = pair_total.astype(jnp.bfloat16).reshape(experts * capacity, width)
    gathered = expert_rows[dest].astype(jnp.float32) * route_weights.reshape(-1)[:, None]
    mixture = jnp.sum(gathered.reshape(tokens, topk, width), axis=1)
    final = (mid_float + mixture).astype(jnp.bfloat16)
    return (mid[None], final[None])


def solution(mesh):
    return jax.shard_map(
        body,
        mesh=mesh,
        in_specs=(
            P("grp", "ctx", None),
            P("grp", "ctx", None),
            P("grp", "ctx", None),
            P("grp", "ctx", None),
            P("grp", None),
            P(),
            P("ctx", None),
            P(),
            P(),
            P("grp", "ctx", None),
            P(("ctx", "grp"), None, None),
            P(("ctx", "grp"), None, None),
        ),
        out_specs=(P("grp", "ctx", None), P("grp", "ctx", None)),
        check_vma=False,
    )
```

profile of v0, /device:TPU:1, one launch (start us, length us, event | category | flops | bytes accessed | tf_op | source)
XLA Modules:
  0.0 733.3 jit_solution(131095022201304216)
XLA Ops:
  14.6 98.2 %all-gather.3.cloned.1.call-done = bf16[6144,1024]{0,1:T(8,128)(2,1)} async-done(((bf16[384,1024]{0,1:T(8,128)(2,1)}), bf16[6144,1024]{0,1:T(8,128)(2,1)}) %all-gather.3.cloned.1.call-update) | async-done | bytes 12582928 | tf_op jit(solution)/shard_map/all_gather | solution.py:92
  112.8 157.6 %while.20 = (s32[]{:T(128)}, f32[8,4,128]{2,1,0:T(4,128)S(1)}, f32[8,4,128]{2,1,0:T(4,128)S(1)}, f32[8,4,128,64]{2,3,1,0:T(8,128)S(1)}, s32[1,8]{1,0:T(1,128)S(1...) while((s32[]{:T(128)}, f32[8,4,128]{2,1,0:T(4,128)S(1)}, ...), condition=%wide.region_7.8_spmd.clone, body=%wide.region_3.7_spmd.clone.sunk | while | flops 1121116288 | bytes 60053240 | solution.py:101
  115.0 7.0 fusion.69
  122.1 9.8 %fusion.70 = f32[8,4,128]{2,1,0:T(4,128)S(1)} fusion(f32[8,1024,128,4]{2,1,3,0:T(8,128)} %get-tuple-element.355, f32[8,4,128]{2,1,0:T(4,128)S(1)} %max.12, pred[128,1024]{0,1:T(8,128)(4,1)S(1)} %compare_and_fusion.2), kind=kLoop, calls=%fused_computation.10.clone.1 | loop fusion | flops 16773120 | bytes 16941056 | tf_op jit(solution)/shard_map/while/body/eval_jaxpr/reduce_sum | solution.py:80
  131.9 7.6 %fusion.72 = f32[8,4,128,64]{2,3,1,0:T(8,128)S(1)} fusion(bf16[1024,8,64,1]{0,2,3,1:T(8,128)(2,1)S(1)} %bitcast.98, f32[8,1024,128,4]{2,1,3,0:T(8,128)} %get-tuple-element.355, f32[8,4,128]{2,1,0:T(4,128)S(1)} %max.12, pred[128,1024]{0,1:T(8,128)(4,1)S(1)} %compare_and_fusion.2, f32[8,4,128,64]{2,3,1,0:T(8,128)S(1)} %get-tuple-element.376, ...), kind=kOutput, calls=%fused_computation.13.clone.1 | convolution fusion | flops 554434560 | bytes 20086784 | tf_op jit(solution)/shard_map/while/body/eval_jaxpr/kgqs,skd->kgqd/dot_general | solution.py:81
  141.8 7.1 fusion.69
  148.9 9.1 %fusion.70 = f32[8,4,128]{2,1,0:T(4,128)S(1)} fusion(f32[8,1024,128,4]{2,1,3,0:T(8,128)} %get-tuple-element.355, f32[8,4,128]{2,1,0:T(4,128)S(1)} %max.12, pred[128,1024]{0,1:T(8,128)(4,1)S(1)} %compare_and_fusion.2), kind=kLoop, calls=%fused_computation.10.clone.1 | loop fusion | flops 16773120 | bytes 16941056 | tf_op jit(solution)/shard_map/while/body/eval_jaxpr/reduce_sum | solution.py:80
  158.0 7.9 %fusion.72 = f32[8,4,128,64]{2,3,1,0:T(8,128)S(1)} fusion(bf16[1024,8,64,1]{0,2,3,1:T(8,128)(2,1)S(1)} %bitcast.98, f32[8,1024,128,4]{2,1,3,0:T(8,128)} %get-tuple-element.355, f32[8,4,128]{2,1,0:T(4,128)S(1)} %max.12, pred[128,1024]{0,1:T(8,128)(4,1)S(1)} %compare_and_fusion.2, f32[8,4,128,64]{2,3,1,0:T(8,128)S(1)} %get-tuple-element.376, ...), kind=kOutput, calls=%fused_computation.13.clone.1 | convolution fusion | flops 554434560 | bytes 20086784 | tf_op jit(solution)/shard_map/while/body/eval_jaxpr/kgqs,skd->kgqd/dot_general | solution.py:81
  168.1 7.2 fusion.69
  175.3 9.8 %fusion.70 = f32[8,4,128]{2,1,0:T(4,128)S(1)} fusion(f32[8,1024,128,4]{2,1,3,0:T(8,128)} %get-tuple-element.355, f32[8,4,128]{2,1,0:T(4,128)S(1)} %max.12, pred[128,1024]{0,1:T(8,128)(4,1)S(1)} %compare_and_fusion.2), kind=kLoop, calls=%fused_computation.10.clone.1 | loop fusion | flops 16773120 | bytes 16941056 | tf_op jit(solution)/shard_map/while/body/eval_jaxpr/reduce_sum | solution.py:80
  185.1 7.4 %fusion.72 = f32[8,4,128,64]{2,3,1,0:T(8,128)S(1)} fusion(bf16[1024,8,64,1]{0,2,3,1:T(8,128)(2,1)S(1)} %bitcast.98, f32[8,1024,128,4]{2,1,3,0:T(8,128)} %get-tuple-element.355, f32[8,4,128]{2,1,0:T(4,128)S(1)} %max.12, pred[128,1024]{0,1:T(8,128)(4,1)S(1)} %compare_and_fusion.2, f32[8,4,128,64]{2,3,1,0:T(8,128)S(1)} %get-tuple-element.376, ...), kind=kOutput, calls=%fused_computation.13.clone.1 | convolution fusion | flops 554434560 | bytes 20086784 | tf_op jit(solution)/shard_map/while/body/eval_jaxpr/kgqs,skd->kgqd/dot_general | solution.py:81
  194.8 7.3 fusion.69
  202.1 9.1 %fusion.70 = f32[8,4,128]{2,1,0:T(4,128)S(1)} fusion(f32[8,1024,128,4]{2,1,3,0:T(8,128)} %get-tuple-element.355, f32[8,4,128]{2,1,0:T(4,128)S(1)} %max.12, pred[128,1024]{0,1:T(8,128)(4,1)S(1)} %compare_and_fusion.2), kind=kLoop, calls=%fused_computation.10.clone.1 | loop fusion | flops 16773120 | bytes 16941056 | tf_op jit(solution)/shard_map/while/body/eval_jaxpr/reduce_sum | solution.py:80
  211.2 7.4 %fusion.72 = f32[8,4,128,64]{2,3,1,0:T(8,128)S(1)} fusion(bf16[1024,8,64,1]{0,2,3,1:T(8,128)(2,1)S(1)} %bitcast.98, f32[8,1024,128,4]{2,1,3,0:T(8,128)} %get-tuple-element.355, f32[8,4,128]{2,1,0:T(4,128)S(1)} %max.12, pred[128,1024]{0,1:T(8,128)(4,1)S(1)} %compare_and_fusion.2, f32[8,4,128,64]{2,3,1,0:T(8,128)S(1)} %get-tuple-element.376, ...), kind=kOutput, calls=%fused_computation.13.clone.1 | convolution fusion | flops 554434560 | bytes 20086784 | tf_op jit(solution)/shard_map/while/body/eval_jaxpr/kgqs,skd->kgqd/dot_general | solution.py:81
  227.9 9.1 %fusion.70 = f32[8,4,128]{2,1,0:T(4,128)S(1)} fusion(f32[8,1024,128,4]{2,1,3,0:T(8,128)} %get-tuple-element.355, f32[8,4,128]{2,1,0:T(4,128)S(1)} %max.12, pred[128,1024]{0,1:T(8,128)(4,1)S(1)} %compare_and_fusion.2), kind=kLoop, calls=%fused_computation.10.clone.1 | loop fusion | flops 16773120 | bytes 16941056 | tf_op jit(solution)/shard_map/while/body/eval_jaxpr/reduce_sum | solution.py:80
  237.0 7.4 %fusion.72 = f32[8,4,128,64]{2,3,1,0:T(8,128)S(1)} fusion(bf16[1024,8,64,1]{0,2,3,1:T(8,128)(2,1)S(1)} %bitcast.98, f32[8,1024,128,4]{2,1,3,0:T(8,128)} %get-tuple-element.355, f32[8,4,128]{2,1,0:T(4,128)S(1)} %max.12, pred[128,1024]{0,1:T(8,128)(4,1)S(1)} %compare_and_fusion.2, f32[8,4,128,64]{2,3,1,0:T(8,128)S(1)} %get-tuple-element.376, ...), kind=kOutput, calls=%fused_computation.13.clone.1 | convolution fusion | flops 554434560 | bytes 20086784 | tf_op jit(solution)/shard_map/while/body/eval_jaxpr/kgqs,skd->kgqd/dot_general | solution.py:81
  253.7 9.1 %fusion.70 = f32[8,4,128]{2,1,0:T(4,128)S(1)} fusion(f32[8,1024,128,4]{2,1,3,0:T(8,128)} %get-tuple-element.355, f32[8,4,128]{2,1,0:T(4,128)S(1)} %max.12, pred[128,1024]{0,1:T(8,128)(4,1)S(1)} %compare_and_fusion.2), kind=kLoop, calls=%fused_computation.10.clone.1 | loop fusion | flops 16773120 | bytes 16941056 | tf_op jit(solution)/shard_map/while/body/eval_jaxpr/reduce_sum | solution.py:80
  262.8 7.4 %fusion.72 = f32[8,4,128,64]{2,3,1,0:T(8,128)S(1)} fusion(bf16[1024,8,64,1]{0,2,3,1:T(8,128)(2,1)S(1)} %bitcast.98, f32[8,1024,128,4]{2,1,3,0:T(8,128)} %get-tuple-element.355, f32[8,4,128]{2,1,0:T(4,128)S(1)} %max.12, pred[128,1024]{0,1:T(8,128)(4,1)S(1)} %compare_and_fusion.2, f32[8,4,128,64]{2,3,1,0:T(8,128)S(1)} %get-tuple-element.376, ...), kind=kOutput, calls=%fused_computation.13.clone.1 | convolution fusion | flops 554434560 | bytes 20086784 | tf_op jit(solution)/shard_map/while/body/eval_jaxpr/kgqs,skd->kgqd/dot_general | solution.py:81
  270.7 7.7 %fusion.35 = (f32[128]{0:T(128)S(1)}, bf16[128,2880]{0,1:T(8,128)(2,1)S(1)}) fusion(bf16[2048,2880]{0,1:T(8,128)(2,1)} %all-gather.5.cloned.1.call-done, bf16[128,2048]{0,1:T(8,128)(2,1)S(1)} %bitcast.102, bf16[1,128,2880]{1,2,0:T(8,128)(2,1)} %param.14), kind=kOutput, calls=%fused_computation.55 | convolution fusion | flops 1512161152 | bytes 13795840 | tf_op jit(solution)/shard_map/dot_general | solution.py:110
  280.1 16.4 %scatter_custom_fusion = bf16[640,2880]{1,0:T(8,128)(2,1)} fusion(s32[512]{0:T(512)S(1)} %bitcast.106, bf16[128,2880]{1,0:T(8,128)(2,1)S(1)} %copy.54, s32[1024]{0:T(1024)S(1)} %pad_clamp_fusion.1, bf16[]{:T(256)} %constant.176.clone.1), kind=kCustom, calls=%fused_computation.47 | custom fusion | bytes 3686402 | tf_op jit(solution)/shard_map/scatter | solution.py:137
  296.5 7.3 broadcast_in_dim.138
  308.3 147.2 %all_to_all.10 = bf16[128,10,2880]{2,1,0:T(8,128)(2,1)} all-to-all(bf16[128,10,2880]{2,1,0:T(8,128)(2,1)S(1)} %bitcast.97), channel_id=1, replica_groups=mesh['ctx'=16,'grp'=8] {'ctx','grp'}, dimensions={0} | all-to-all | bytes 14745600 | tf_op jit(solution)/shard_map/all_to_all | solution.py:145
  455.5 14.4 %reshape.320 = bf16[1280,2880]{1,0:T(8,128)(2,1)} reshape(bf16[128,10,2880]{2,1,0:T(8,128)(2,1)} %all_to_all.10) | data formatting | bytes 14745600 | tf_op jit(solution)/shard_map/reshape | solution.py:146
  469.9 17.2 %fusion.22 = f32[1280,1536]{1,0:T(8,128)S(1)} fusion(bf16[1280,2880]{1,0:T(8,128)(2,1)} %reshape.320, bf16[1,2880,1536]{2,1,0:T(8,128)(2,1)} %param.24), kind=kOutput, calls=%fused_computation.37 | convolution fusion | flops 11324620800 | bytes 24084480 | tf_op jit(solution)/shard_map/dot_general | solution.py:147
  487.2 11.8 %convolution_convert_fusion = bf16[1280,2880]{0,1:T(8,128)(2,1)} fusion(bf16[1,768,2880]{1,2,0:T(8,128)(2,1)} %param.25, f32[1280,1536]{1,0:T(8,128)S(1)} %fusion.22), kind=kOutput, calls=%fused_computation.36 | convolution fusion | flops 5673861120 | bytes 19660800 | tf_op jit(solution)/shard_map/dot_general | solution.py:149
  498.9 10.4 %copy.55 = bf16[1280,2880]{1,0:T(8,128)(2,1)} copy(bf16[1280,2880]{0,1:T(8,128)(2,1)} %convolution_convert_fusion) | data formatting | bytes 14745600 | tf_op jit(solution)/shard_map/convert_element_type | solution.py:149
  509.4 13.4 %reshape.321 = bf16[128,10,2880]{2,1,0:T(8,128)(2,1)} reshape(bf16[1280,2880]{1,0:T(8,128)(2,1)} %copy.55) | data formatting | bytes 14745600 | tf_op jit(solution)/shard_map/reshape | solution.py:152
  522.7 8.2 %all-to-all-start.1 = ((bf16[128,10,2880]{2,1,0:T(8,128)(2,1)}), bf16[128,10,2880]{2,1,0:T(8,128)(2,1)}, u32[]{:S(2)}, u32[]{:S(2)}) async-start(bf16[128,10,2880]{2,1,0:T(8,128)(2,1)} %reshape.321), calls=%async_computation.1 | async-start | bytes 24117248 | tf_op jit(solution)/shard_map/all_to_all | solution.py:153
  531.4 150.6 %all-to-all-done.1 = bf16[128,10,2880]{2,1,0:T(8,128)(2,1)} async-done(((bf16[128,10,2880]{2,1,0:T(8,128)(2,1)}), bf16[128,10,2880]{2,1,0:T(8,128)(2,1)}, u32[]{:S(2)}, u32[]{:S(2)}) %all-to-all-start.1) | async-done | bytes 7372832 | tf_op jit(solution)/shard_map/all_to_all | solution.py:153
  682.1 14.7 %bitcast_reduce_fusion = bf16[64,10,2880]{2,1,0:T(8,128)(2,1)} fusion(bf16[128,10,2880]{2,1,0:T(8,128)(2,1)} %all-to-all-done.1), kind=kLoop, calls=%fused_computation.35 | loop fusion | flops 1843200 | bytes 11059200 | tf_op jit(solution)/shard_map/reduce_sum | solution.py:154
  696.8 7.8 %reshape.323 = bf16[640,2880]{1,0:T(8,128)(2,1)} reshape(bf16[64,10,2880]{2,1,0:T(8,128)(2,1)} %bitcast_reduce_fusion) | data formatting | bytes 7372800 | tf_op jit(solution)/shard_map/reshape | solution.py:155
  704.5 8.4 %gather_fusion = bf16[512,2880]{1,0:T(8,128)(2,1)S(1)} fusion(bf16[640,2880]{1,0:T(8,128)(2,1)} %reshape.323, s32[1024]{0:T(1024)S(1)} %pad_clamp_fusion), kind=kCustom, calls=%fused_computation.1 | custom fusion | bytes 5900288 | tf_op jit(solution)/shard_map/gather | solution.py:156
  (114 shorter events, 54.9 us)
Async XLA Ops:
  7.2 523.8 %copy-start = (bf16[2880,64]{0,1:T(8,128)(2,1)S(1)}, bf16[2880,64]{0,1:T(8,128)(2,1)}, u32[]{:S(2)}) copy-start(bf16[2880,64]{0,1:T(8,128)(2,1)} %param.22) | copy-start | bytes 1105924
  7.2 4.3 copy-start.3
  7.2 4.7 copy-start.6
  7.2 4.8 copy-start.7
  7.2 5.1 copy-start.2
  7.2 105.5 %all-gather.3.cloned.1.call-start = ((), (), s32[]{:S(2)}) async-start(), calls=%async_computation.2 | async-start | bytes 13369344 | tf_op jit(solution)/shard_map/all_gather | solution.py:92
  10.7 260.0 %all-gather.5.cloned.1.call-start = ((), (), s32[]{:S(2)}) async-start(), calls=%async_computation.3 | async-start | bytes 12533760 | tf_op jit(solution)/shard_map/all_gather | solution.py:112
  270.7 8.6 %copy-start.5 = (f32[2880]{0:T(1024)S(1)}, f32[2880]{0:T(1024)}, u32[]{:S(2)}) copy-start(f32[2880]{0:T(1024)} %param.21) | copy-start | bytes 34564
  278.4 0.9 copy-start.1
  522.7 8.5 %copy-start.4 = (s32[1,128,4]{1,2,0:T(4,128)S(1)}, s32[1,128,4]{1,2,0:T(4,128)}, u32[]{:S(2)}) copy-start(s32[1,128,4]{1,2,0:T(4,128)} %param.23) | copy-start | bytes 6148
  522.7 159.3 %all-to-all-start.1 = ((bf16[128,10,2880]{2,1,0:T(8,128)(2,1)}), bf16[128,10,2880]{2,1,0:T(8,128)(2,1)}, u32[]{:S(2)}, u32[]{:S(2)}) async-start(bf16[128,10,2880]{2,1,0:T(8,128)(2,1)} %reshape.321), calls=%async_computation.1 | async-start | bytes 24117248 | tf_op jit(solution)/shard_map/all_to_all | solution.py:153
Sparse Core Ops, SparseCore 0:
  10.8 101.8 all-gather.2
  114.9 94.9 all-gather.4
where the time goes:
time: 747 us; the launch traced here: 733 us
  waiting for transfers between devices  250 us (33%)
  blocking collectives  147 us (20%)
  matrix products  125 us (17%)
  local copies, waits for them, and re-layouts  102 us (14%)
  other arithmetic  86.2 us (12%)
  between operations  14.6 us (2%)
  starting transfers between devices  8.3 us (1%)
    all_to_all x1, waiting for transfers between devices, body(): lax.all_to_all(partial_out, ('ctx', 'grp'), split_axis=0, concat_axis=0,...  151 us
    all_to_all x1, blocking collectives, body(): lax.all_to_all(doubled, ('ctx', 'grp'), split_axis=0, concat_axis=0, tile...  147 us
    all_gather x1, waiting for transfers between devices, body(): piece = lax.all_gather(local_kv, 'ctx', axis=0, tiled=True)  98.2 us
    reduce_sum x6, other arithmetic, key_block(): total = total * shrink + jnp.sum(weights, axis=-1)  55.9 us
    dot_general x6, matrix products, key_block(): jnp.einsum('kgqs,skd->kgqd', weights.astype(jnp.bfloat16), values, prefer...  45.1 us
    dot_general x6, matrix products, key_block(): jnp.einsum('qkgd,skd->kgqs', query_heads, keys, preferred_element_type=jn...  42.7 us
    dot_general x1, matrix products, body(): pre = jnp.dot(flat_rows, in_weights, preferred_element_type=jnp.float32)  17.2 us
    scatter x1, local copies, waits for them, and re-layouts, body(): jnp.zeros((experts * capacity, width), jnp.bfloat16).at[dest]  16.4 us
  transfers between devices with their start and end apart: 3, of which 2 were waited for; matrix products, arithmetic and copies ran while one was open for 22% of the time, Pallas kernels for 0%

commit v1 on v0

--- a/solution.py
+++ b/solution.py
@@ -107,11 +107,23 @@
         .reshape(tokens, HEADS * HD)
         .astype(jnp.bfloat16)
     )
-    projected = jnp.dot(
-        attended,
-        lax.all_gather(out_proj, "ctx", axis=0, tiled=True),
-        preferred_element_type=jnp.float32,
+    grp_here = lax.axis_index("grp")
+    parity = grp_here % 2
+    grp_count = lax.axis_size("grp")
+    pair_perm = [(g, g ^ 1) for g in range(grp_count)]
+    head_rows = out_proj.shape[0] // 2
+    proj_half = lax.all_gather(
+        lax.dynamic_slice_in_dim(out_proj, parity * head_rows, head_rows, 0), "ctx", axis=0, tiled=True
     )
+    by_parity = attended.reshape(tokens, HEADS // 2, 2, HD)
+    mine = jnp.where(parity == 0, by_parity[:, :, 0], by_parity[:, :, 1]).reshape(tokens, -1)
+    theirs_cols = jnp.where(parity == 0, by_parity[:, :, 1], by_parity[:, :, 0]).reshape(tokens, -1)
+    partner_cols = lax.ppermute(theirs_cols, "grp", pair_perm)
+    both = jnp.dot(
+        jnp.concatenate([mine, partner_cols], axis=0), proj_half, preferred_element_type=jnp.float32
+    )
+    back = lax.ppermute(both[tokens:], "grp", pair_perm)
+    projected = both[:tokens] + back
     mid = (residual[0].astype(jnp.float32) + projected).astype(jnp.bfloat16)
     mid_float = mid.astype(jnp.float32)
     normed = (
@@ -139,20 +151,25 @@
     in_weights = expert_in[0]
     out_weights = expert_out[0]
     half_width = out_weights.shape[0]
-    doubled = jnp.broadcast_to(packed[:, None], (experts, 2, capacity, width)).reshape(
-        2 * experts, capacity, width
+    owners = 2 * experts
+    half_cap = capacity // 2
+    split = packed.reshape(owners, half_cap, width)
+    received = lax.all_to_all(split, ("ctx", "grp"), split_axis=0, concat_axis=0, tiled=True)
+    partner_rows = lax.ppermute(received, "grp", pair_perm)
+
+    def expert_half(rows):
+        pre = jnp.dot(rows.reshape(-1, width), in_weights, preferred_element_type=jnp.float32)
+        hidden = gated_act(pre, half_width)
+        return jnp.dot(hidden, out_weights, preferred_element_type=jnp.float32).astype(jnp.bfloat16)
+
+    own_part = expert_half(received)
+    partner_part = expert_half(partner_rows)
+    partner_back = lax.ppermute(partner_part, "grp", pair_perm)
+    summed = (own_part.astype(jnp.float32) + partner_back.astype(jnp.float32)).astype(jnp.bfloat16)
+    returned = lax.all_to_all(
+        summed.reshape(owners, half_cap, width), ("ctx", "grp"), split_axis=0, concat_axis=0, tiled=True
     )
-    received = lax.all_to_all(doubled, ("ctx", "grp"), split_axis=0, concat_axis=0, tiled=True)
-    flat_rows = received.reshape(-1, width)
-    pre = jnp.dot(flat_rows, in_weights, preferred_element_type=jnp.float32)
-    hidden = gated_act(pre, half_width)
-    partial_out = jnp.dot(hidden, out_weights, preferred_element_type=jnp.float32).astype(
-        jnp.bfloat16
-    )
-    partial_out = partial_out.reshape(received.shape)
-    returned = lax.all_to_all(partial_out, ("ctx", "grp"), split_axis=0, concat_axis=0, tiled=True)
-    pair_total = jnp.sum(returned.reshape(experts, 2, capacity, width).astype(jnp.float32), axis=1)
-    expert_rows = pair_total.astype(jnp.bfloat16).reshape(experts * capacity, width)
+    expert_rows = returned.reshape(experts * capacity, width)
     gathered = expert_rows[dest].astype(jnp.float32) * route_weights.reshape(-1)[:, None]
     mixture = jnp.sum(gathered.reshape(tokens, topk, width), axis=1)
     final = (mid_float + mixture).astype(jnp.bfloat16)

time: 747 us -> 613 us (0.82)
  waiting for transfers between devices: 250 us -> 181 us
  blocking collectives: 147 us -> 80.1 us
  other arithmetic: 86.2 us -> 72.8 us
  local copies, waits for them, and re-layouts: 102 us -> 114 us
    all_to_all x1, waiting for transfers between devices: 151 us -> 73.2 us  [body(): lax.all_to_all(summed.reshape(owners, half_cap, width), ('ctx', 'grp'), s...]
    all_to_all x1, blocking collectives: 147 us -> 80.1 us  [body(): lax.all_to_all(split, ('ctx', 'grp'), split_axis=0, concat_axis=0, tiled=...]
    reduce_sum x1, other arithmetic: 14.7 us -> 1.96 us  [body(): jnp.mean(mid_float * mid_float, axis=-1, keepdims=True) + 1e-05]
    broadcast_in_dim x2 -> x0, local copies, waits for them, and re-layouts: 11.8 us -> none  [body(): jnp.broadcast_to(packed[:, None], (experts, 2, capacity, width))]
    ppermute x0 -> x1, local copies, waits for them, and re-layouts: none -> 8.47 us  [body(): partner_rows = lax.ppermute(received, 'grp', pair_perm)]
    ppermute x0 -> x4, waiting for transfers between devices: none -> 8.45 us  [the longest x1 6.4 us: body(): partner_rows = lax.ppermute(received, 'grp', pair_perm)]
    all_to_all x0 -> x1, local copies, waits for them, and re-layouts: none -> 7.88 us  [body(): lax.all_to_all(split, ('ctx', 'grp'), split_axis=0, concat_axis=0, tiled=...]
    dot_general x3 -> x5, matrix products: 36.7 us -> 41.8 us  [the longest x2 19.7 us: expert_half(): jnp.dot(rows.reshape(-1, width), in_weights, preferred_element_type=jnp.f...]
  transfers between devices with their start and end apart: 3 -> 7, of which waited for: 2 -> 5; matrix products, arithmetic and copies ran while one was open for 22% -> 30% of each run, Pallas kernels for 0% -> 0%
where the time goes in v1:
time: 613 us; the launch traced here: 602 us
  waiting for transfers between devices  181 us (30%)
  matrix products  130 us (21%)
  local copies, waits for them, and re-layouts  114 us (19%)
  blocking collectives  80.1 us (13%)
  other arithmetic  72.8 us (12%)
  between operations  14.9 us (2%)
  starting transfers between devices  9.35 us (2%)
    all_gather x1, waiting for transfers between devices, body(): piece = lax.all_gather(local_kv, 'ctx', axis=0, tiled=True)  99.8 us
    all_to_all x1, blocking collectives, body(): lax.all_to_all(split, ('ctx', 'grp'), split_axis=0, concat_axis=0, tiled=...  80.1 us
    all_to_all x1, waiting for transfers between devices, body(): lax.all_to_all(summed.reshape(owners, half_cap, width), ('ctx', 'grp'), s...  73.2 us
    reduce_sum x6, other arithmetic, key_block(): total = total * shrink + jnp.sum(weights, axis=-1)  54.9 us
    dot_general x6, matrix products, key_block(): jnp.einsum('kgqs,skd->kgqd', weights.astype(jnp.bfloat16), values, prefer...  44.9 us
    dot_general x6, matrix products, key_block(): jnp.einsum('qkgd,skd->kgqs', query_heads, keys, preferred_element_type=jn...  42.6 us
    dot_general x2, matrix products, expert_half(): jnp.dot(rows.reshape(-1, width), in_weights, preferred_element_type=jnp.f...  19.7 us
    dot_general x2, matrix products, expert_half(): jnp.dot(hidden, out_weights, preferred_element_type=jnp.float32)  16.8 us
  transfers between devices with their start and end apart: 7, of which 5 were waited for; matrix products, arithmetic and copies ran while one was open for 30% of the time, Pallas kernels for 0%

profile of v1, /device:TPU:1, one launch (start us, length us, event | category | flops | bytes accessed | tf_op | source)
XLA Modules:
  0.0 602.3 jit_solution(10687653311530739906)
XLA Ops:
  12.9 99.8 %all-gather.3.cloned.1.call-done = bf16[6144,1024]{0,1:T(8,128)(2,1)} async-done(((bf16[384,1024]{0,1:T(8,128)(2,1)}), bf16[6144,1024]{0,1:T(8,128)(2,1)}) %all-gather.3.cloned.1.call-update) | async-done | bytes 12582928 | tf_op jit(solution)/shard_map/all_gather | solution.py:92
  112.8 156.1 %while.20 = (s32[]{:T(128)}, f32[8,4,128]{2,1,0:T(4,128)S(1)}, f32[8,4,128]{2,1,0:T(4,128)S(1)}, f32[8,4,128,64]{2,3,1,0:T(8,128)S(1)}, s32[1,8]{1,0:T(1,128)S(1...) while((s32[]{:T(128)}, f32[8,4,128]{2,1,0:T(4,128)S(1)}, ...), condition=%wide.region_7.8_spmd.clone, body=%wide.region_3.7_spmd.clone.sunk | while | flops 1121116288 | bytes 60053240 | solution.py:101
  115.0 7.0 %fusion.89 = (f32[8,4,128]{2,1,0:T(4,128)S(1)}, f32[8,1024,128,4]{2,1,3,0:T(8,128)}) fusion(pred[128,1024]{0,1:T(8,128)(4,1)S(1)} %compare_and_fusion.2, bf16[1024,8,64,1]{0,2,3,1:T(8,128)(2,1)S(1)} %bitcast.101, bf16[128,8,4,64]{0,3,2,1:T(8,128)(2,1)S(1)} %get-tuple-element.396), kind=kOutput, calls=%fused_computation.6.clone.1 | convolution fusion | flops 549449728 | bytes 18497536 | tf_op jit(solution)/shard_map/while/body/eval_jaxpr/qkgd,skd->kgqs/dot_general | solution.py:73
  122.0 9.5 %fusion.90 = f32[8,4,128]{2,1,0:T(4,128)S(1)} fusion(f32[8,1024,128,4]{2,1,3,0:T(8,128)} %get-tuple-element.357, f32[8,4,128]{2,1,0:T(4,128)S(1)} %max.12, pred[128,1024]{0,1:T(8,128)(4,1)S(1)} %compare_and_fusion.2), kind=kLoop, calls=%fused_computation.10.clone.1 | loop fusion | flops 16773120 | bytes 16941056 | tf_op jit(solution)/shard_map/while/body/eval_jaxpr/reduce_sum | solution.py:80
  131.6 7.6 %fusion.92 = f32[8,4,128,64]{2,3,1,0:T(8,128)S(1)} fusion(bf16[1024,8,64,1]{0,2,3,1:T(8,128)(2,1)S(1)} %bitcast.103, f32[8,1024,128,4]{2,1,3,0:T(8,128)} %get-tuple-element.357, f32[8,4,128]{2,1,0:T(4,128)S(1)} %max.12, pred[128,1024]{0,1:T(8,128)(4,1)S(1)} %compare_and_fusion.2, f32[8,4,128,64]{2,3,1,0:T(8,128)S(1)} %get-tuple-element.378, ...), kind=kOutput, calls=%fused_computation.13.clone.1 | convolution fusion | flops 554434560 | bytes 20086784 | tf_op jit(solution)/shard_map/while/body/eval_jaxpr/kgqs,skd->kgqd/dot_general | solution.py:81
  141.3 7.3 %fusion.89 = (f32[8,4,128]{2,1,0:T(4,128)S(1)}, f32[8,1024,128,4]{2,1,3,0:T(8,128)}) fusion(pred[128,1024]{0,1:T(8,128)(4,1)S(1)} %compare_and_fusion.2, bf16[1024,8,64,1]{0,2,3,1:T(8,128)(2,1)S(1)} %bitcast.101, bf16[128,8,4,64]{0,3,2,1:T(8,128)(2,1)S(1)} %get-tuple-element.396), kind=kOutput, calls=%fused_computation.6.clone.1 | convolution fusion | flops 549449728 | bytes 18497536 | tf_op jit(solution)/shard_map/while/body/eval_jaxpr/qkgd,skd->kgqs/dot_general | solution.py:73
  148.7 9.1 %fusion.90 = f32[8,4,128]{2,1,0:T(4,128)S(1)} fusion(f32[8,1024,128,4]{2,1,3,0:T(8,128)} %get-tuple-element.357, f32[8,4,128]{2,1,0:T(4,128)S(1)} %max.12, pred[128,1024]{0,1:T(8,128)(4,1)S(1)} %compare_and_fusion.2), kind=kLoop, calls=%fused_computation.10.clone.1 | loop fusion | flops 16773120 | bytes 16941056 | tf_op jit(solution)/shard_map/while/body/eval_jaxpr/reduce_sum | solution.py:80
  157.8 7.7 %fusion.92 = f32[8,4,128,64]{2,3,1,0:T(8,128)S(1)} fusion(bf16[1024,8,64,1]{0,2,3,1:T(8,128)(2,1)S(1)} %bitcast.103, f32[8,1024,128,4]{2,1,3,0:T(8,128)} %get-tuple-element.357, f32[8,4,128]{2,1,0:T(4,128)S(1)} %max.12, pred[128,1024]{0,1:T(8,128)(4,1)S(1)} %compare_and_fusion.2, f32[8,4,128,64]{2,3,1,0:T(8,128)S(1)} %get-tuple-element.378, ...), kind=kOutput, calls=%fused_computation.13.clone.1 | convolution fusion | flops 554434560 | bytes 20086784 | tf_op jit(solution)/shard_map/while/body/eval_jaxpr/kgqs,skd->kgqd/dot_general | solution.py:81
  167.8 7.0 %fusion.89 = (f32[8,4,128]{2,1,0:T(4,128)S(1)}, f32[8,1024,128,4]{2,1,3,0:T(8,128)}) fusion(pred[128,1024]{0,1:T(8,128)(4,1)S(1)} %compare_and_fusion.2, bf16[1024,8,64,1]{0,2,3,1:T(8,128)(2,1)S(1)} %bitcast.101, bf16[128,8,4,64]{0,3,2,1:T(8,128)(2,1)S(1)} %get-tuple-element.396), kind=kOutput, calls=%fused_computation.6.clone.1 | convolution fusion | flops 549449728 | bytes 18497536 | tf_op jit(solution)/shard_map/while/body/eval_jaxpr/qkgd,skd->kgqs/dot_general | solution.py:73
  174.9 9.1 %fusion.90 = f32[8,4,128]{2,1,0:T(4,128)S(1)} fusion(f32[8,1024,128,4]{2,1,3,0:T(8,128)} %get-tuple-element.357, f32[8,4,128]{2,1,0:T(4,128)S(1)} %max.12, pred[128,1024]{0,1:T(8,128)(4,1)S(1)} %compare_and_fusion.2), kind=kLoop, calls=%fused_computation.10.clone.1 | loop fusion | flops 16773120 | bytes 16941056 | tf_op jit(solution)/shard_map/while/body/eval_jaxpr/reduce_sum | solution.py:80
  184.0 7.4 %fusion.92 = f32[8,4,128,64]{2,3,1,0:T(8,128)S(1)} fusion(bf16[1024,8,64,1]{0,2,3,1:T(8,128)(2,1)S(1)} %bitcast.103, f32[8,1024,128,4]{2,1,3,0:T(8,128)} %get-tuple-element.357, f32[8,4,128]{2,1,0:T(4,128)S(1)} %max.12, pred[128,1024]{0,1:T(8,128)(4,1)S(1)} %compare_and_fusion.2, f32[8,4,128,64]{2,3,1,0:T(8,128)S(1)} %get-tuple-element.378, ...), kind=kOutput, calls=%fused_computation.13.clone.1 | convolution fusion | flops 554434560 | bytes 20086784 | tf_op jit(solution)/shard_map/while/body/eval_jaxpr/kgqs,skd->kgqd/dot_general | solution.py:81
  200.7 9.1 %fusion.90 = f32[8,4,128]{2,1,0:T(4,128)S(1)} fusion(f32[8,1024,128,4]{2,1,3,0:T(8,128)} %get-tuple-element.357, f32[8,4,128]{2,1,0:T(4,128)S(1)} %max.12, pred[128,1024]{0,1:T(8,128)(4,1)S(1)} %compare_and_fusion.2), kind=kLoop, calls=%fused_computation.10.clone.1 | loop fusion | flops 16773120 | bytes 16941056 | tf_op jit(solution)/shard_map/while/body/eval_jaxpr/reduce_sum | solution.py:80
  209.8 7.4 %fusion.92 = f32[8,4,128,64]{2,3,1,0:T(8,128)S(1)} fusion(bf16[1024,8,64,1]{0,2,3,1:T(8,128)(2,1)S(1)} %bitcast.103, f32[8,1024,128,4]{2,1,3,0:T(8,128)} %get-tuple-element.357, f32[8,4,128]{2,1,0:T(4,128)S(1)} %max.12, pred[128,1024]{0,1:T(8,128)(4,1)S(1)} %compare_and_fusion.2, f32[8,4,128,64]{2,3,1,0:T(8,128)S(1)} %get-tuple-element.378, ...), kind=kOutput, calls=%fused_computation.13.clone.1 | convolution fusion | flops 554434560 | bytes 20086784 | tf_op jit(solution)/shard_map/while/body/eval_jaxpr/kgqs,skd->kgqd/dot_general | solution.py:81
  226.5 9.1 %fusion.90 = f32[8,4,128]{2,1,0:T(4,128)S(1)} fusion(f32[8,1024,128,4]{2,1,3,0:T(8,128)} %get-tuple-element.357, f32[8,4,128]{2,1,0:T(4,128)S(1)} %max.12, pred[128,1024]{0,1:T(8,128)(4,1)S(1)} %compare_and_fusion.2), kind=kLoop, calls=%fused_computation.10.clone.1 | loop fusion | flops 16773120 | bytes 16941056 | tf_op jit(solution)/shard_map/while/body/eval_jaxpr/reduce_sum | solution.py:80
  235.6 7.4 %fusion.92 = f32[8,4,128,64]{2,3,1,0:T(8,128)S(1)} fusion(bf16[1024,8,64,1]{0,2,3,1:T(8,128)(2,1)S(1)} %bitcast.103, f32[8,1024,128,4]{2,1,3,0:T(8,128)} %get-tuple-element.357, f32[8,4,128]{2,1,0:T(4,128)S(1)} %max.12, pred[128,1024]{0,1:T(8,128)(4,1)S(1)} %compare_and_fusion.2, f32[8,4,128,64]{2,3,1,0:T(8,128)S(1)} %get-tuple-element.378, ...), kind=kOutput, calls=%fused_computation.13.clone.1 | convolution fusion | flops 554434560 | bytes 20086784 | tf_op jit(solution)/shard_map/while/body/eval_jaxpr/kgqs,skd->kgqd/dot_general | solution.py:81
  252.3 9.1 %fusion.90 = f32[8,4,128]{2,1,0:T(4,128)S(1)} fusion(f32[8,1024,128,4]{2,1,3,0:T(8,128)} %get-tuple-element.357, f32[8,4,128]{2,1,0:T(4,128)S(1)} %max.12, pred[128,1024]{0,1:T(8,128)(4,1)S(1)} %compare_and_fusion.2), kind=kLoop, calls=%fused_computation.10.clone.1 | loop fusion | flops 16773120 | bytes 16941056 | tf_op jit(solution)/shard_map/while/body/eval_jaxpr/reduce_sum | solution.py:80
  261.5 7.4 %fusion.92 = f32[8,4,128,64]{2,3,1,0:T(8,128)S(1)} fusion(bf16[1024,8,64,1]{0,2,3,1:T(8,128)(2,1)S(1)} %bitcast.103, f32[8,1024,128,4]{2,1,3,0:T(8,128)} %get-tuple-element.357, f32[8,4,128]{2,1,0:T(4,128)S(1)} %max.12, pred[128,1024]{0,1:T(8,128)(4,1)S(1)} %compare_and_fusion.2, f32[8,4,128,64]{2,3,1,0:T(8,128)S(1)} %get-tuple-element.378, ...), kind=kOutput, calls=%fused_computation.13.clone.1 | convolution fusion | flops 554434560 | bytes 20086784 | tf_op jit(solution)/shard_map/while/body/eval_jaxpr/kgqs,skd->kgqd/dot_general | solution.py:81
  286.7 16.3 %scatter_custom_fusion = bf16[640,2880]{1,0:T(8,128)(2,1)} fusion(s32[512]{0:T(512)S(1)} %bitcast.113, bf16[128,2880]{1,0:T(8,128)(2,1)S(1)} %copy.59, s32[1024]{0:T(1024)S(1)} %pad_clamp_fusion.1, bf16[]{:T(256)} %constant.192.clone.1), kind=kCustom, calls=%fused_computation.45 | custom fusion | bytes 3686402 | tf_op jit(solution)/shard_map/scatter | solution.py:149
  303.0 7.4 %reshape_reshape.3 = bf16[128,5,2880]{2,1,0:T(8,128)(2,1)} reshape(bf16[640,2880]{1,0:T(8,128)(2,1)} %scatter_custom_fusion) | data formatting | bytes 7372800 | tf_op jit(solution)/shard_map/reshape;reshape | solution.py:156
  310.3 80.1 %all_to_all.10 = bf16[128,5,2880]{2,1,0:T(8,128)(2,1)} all-to-all(bf16[128,5,2880]{2,1,0:T(8,128)(2,1)} %reshape_reshape.3), channel_id=1, replica_groups=mesh['ctx'=16,'grp'=8] {'ctx','grp'}, dimensions={0} | all-to-all | bytes 7372800 | tf_op jit(solution)/shard_map/all_to_all | solution.py:157
  390.4 7.9 %copy.60 = bf16[128,5,2880]{0,2,1:T(8,128)(2,1)} copy(bf16[128,5,2880]{2,1,0:T(8,128)(2,1)} %all_to_all.10) | data formatting | bytes 7372800 | tf_op jit(solution)/shard_map/all_to_all | solution.py:157
  406.0 8.5 %copy.61 = bf16[128,5,2880]{2,1,0:T(8,128)(2,1)} copy(bf16[128,5,2880]{0,2,1:T(8,128)(2,1)} %collective-permute-done.2) | data formatting | bytes 7372800 | tf_op jit(solution)/shard_map/ppermute | solution.py:158
  414.4 8.0 %reshape.328 = bf16[640,2880]{1,0:T(8,128)(2,1)} reshape(bf16[128,5,2880]{2,1,0:T(8,128)(2,1)} %copy.61) | data formatting | bytes 7372800 | tf_op jit(solution)/shard_map/reshape | solution.py:161
  422.5 9.9 %fusion.22 = f32[640,1536]{1,0:T(8,128)S(1)} fusion(bf16[640,2880]{1,0:T(8,128)(2,1)} %reshape.328, bf16[1,2880,1536]{2,1,0:T(8,128)(2,1)} %param.24), kind=kOutput, calls=%fused_computation.35 | convolution fusion | flops 5662310400 | bytes 16465920 | tf_op jit(solution)/shard_map/dot_general | solution.py:161
  432.3 7.9 %convolution_convert_fusion = bf16[640,2880]{0,1:T(8,128)(2,1)} fusion(bf16[1,768,2880]{1,2,0:T(8,128)(2,1)} %param.25, f32[640,1536]{1,0:T(8,128)S(1)} %fusion.22), kind=kOutput, calls=%fused_computation.41 | convolution fusion | flops 2836930560 | bytes 12042240 | tf_op jit(solution)/shard_map/dot_general | solution.py:163
  440.6 8.2 %reshape.327 = bf16[640,2880]{1,0:T(8,128)(2,1)} reshape(bf16[128,5,2880]{2,1,0:T(8,128)(2,1)} %all_to_all.10) | data formatting | bytes 7372800 | tf_op jit(solution)/shard_map/reshape | solution.py:161
  448.7 9.9 %fusion.24 = f32[640,1536]{1,0:T(8,128)S(1)} fusion(bf16[640,2880]{1,0:T(8,128)(2,1)} %reshape.327, bf16[1,2880,1536]{2,1,0:T(8,128)(2,1)} %param.24), kind=kOutput, calls=%fused_computation.37 | convolution fusion | flops 5662310400 | bytes 16465920 | tf_op jit(solution)/shard_map/dot_general | solution.py:161
  458.6 9.0 %add_convert_fusion = bf16[640,2880]{0,1:T(8,128)(2,1)} fusion(bf16[640,2880]{0,1:T(8,128)(2,1)} %collective-permute-done.3, bf16[1,768,2880]{1,2,0:T(8,128)(2,1)} %param.25, f32[640,1536]{1,0:T(8,128)S(1)} %fusion.24), kind=kOutput, calls=%fused_computation.39 | convolution fusion | flops 2844303360 | bytes 15728640 | tf_op jit(solution)/shard_map/dot_general | solution.py:163
  473.8 7.4 %reshape.329 = bf16[128,5,2880]{2,1,0:T(8,128)(2,1)} reshape(bf16[640,2880]{1,0:T(8,128)(2,1)} %copy.62) | data formatting | bytes 7372800 | tf_op jit(solution)/shard_map/reshape | solution.py:170
  486.9 73.2 %all-to-all-done.1 = bf16[128,5,2880]{2,1,0:T(8,128)(2,1)} async-done(((bf16[128,5,2880]{2,1,0:T(8,128)(2,1)}), bf16[128,5,2880]{2,1,0:T(8,128)(2,1)}, u32[]{:S(2)}, u32[]{:S(2)}) %all-to-all-start.1) | async-done | bytes 3686432 | tf_op jit(solution)/shard_map/all_to_all | solution.py:169
  560.1 8.0 %reshape.330 = bf16[640,2880]{1,0:T(8,128)(2,1)} reshape(bf16[128,5,2880]{2,1,0:T(8,128)(2,1)} %all-to-all-done.1) | data formatting | bytes 7372800 | tf_op jit(solution)/shard_map/reshape | solution.py:172
  568.1 9.3 %gather_fusion = bf16[512,2880]{1,0:T(8,128)(2,1)} fusion(bf16[640,2880]{1,0:T(8,128)(2,1)} %reshape.330, s32[1024]{0:T(1024)S(1)} %pad_clamp_fusion), kind=kCustom, calls=%fused_computation.1 | custom fusion | bytes 5900288 | tf_op jit(solution)/shard_map/gather | solution.py:173
  (134 shorter events, 95.3 us)
Async XLA Ops:
  7.2 3.6 copy-start
  7.2 4.9 copy-start.9
  7.2 5.3 copy-start.8
  7.2 5.4 copy-start.4
  7.2 105.5 %all-gather.3.cloned.1.call-start = ((), (), s32[]{:S(2)}) async-start(), calls=%async_computation.2 | async-start | bytes 13369344 | tf_op jit(solution)/shard_map/all_gather | solution.py:92
  10.7 260.0 %all-gather.5.cloned.1.call-start = ((), (), s32[]{:S(2)}) async-start(), calls=%async_computation.3 | async-start | bytes 6406144 | tf_op jit(solution)/shard_map/all_gather | solution.py:115
  269.2 2.7 collective-permute-start
  271.9 8.9 %copy-start.6 = (s32[1,128,4]{1,2,0:T(4,128)S(1)}, s32[1,128,4]{1,2,0:T(4,128)}, u32[]{:S(2)}) copy-start(s32[1,128,4]{1,2,0:T(4,128)} %param.23) | copy-start | bytes 6148
  277.2 1.6 copy-start.3
  278.7 7.1 %copy-start.7 = (f32[2880]{0:T(1024)S(1)}, f32[2880]{0:T(1024)}, u32[]{:S(2)}) copy-start(f32[2880]{0:T(1024)} %param.21) | copy-start | bytes 34564
  280.0 3.9 collective-permute-start.1
  285.9 306.7 %copy-start.2 = (bf16[128,2880]{0,1:T(8,128)(2,1)}, bf16[128,2880]{0,1:T(8,128)(2,1)S(1)}, u32[]{:S(2)}) copy-start(bf16[128,2880]{0,1:T(8,128)(2,1)S(1)} %get-tuple-element.287) | copy-start | bytes 2211844
  398.3 7.7 %collective-permute-start.2 = (bf16[128,5,2880]{0,2,1:T(8,128)(2,1)}, bf16[128,5,2880]{0,2,1:T(8,128)(2,1)}, u32[]{:S(2)}, u32[]{:S(2)}) collective-permute-start(bf16[128,5,2880]{0,2,1:T(8,128)(2,1)} %copy.60), channel_id=1, source_target_pairs={{0,1},{1,0},{2,3},{3,2},{4,5},{5,4},{6,7},{7,6},{8,9},{9,8},{10,11... | collective-permute-start | bytes 11059208 | tf_op jit(solution)/shard_map/ppermute | solution.py:158
  440.2 18.4 %collective-permute-start.3 = (bf16[640,2880]{0,1:T(8,128)(2,1)}, bf16[640,2880]{0,1:T(8,128)(2,1)}, u32[]{:S(2)}, u32[]{:S(2)}) collective-permute-start(bf16[640,2880]{0,1:T(8,128)(2,1)} %convolution_convert_fusion), channel_id=1, source_target_pairs={{0,1},{1,0},{2,3},{3,2},{4,5},{5,4},{6,7},{7,6},{8,9},{9,8},{10,11... | collective-permute-start | bytes 11059208 | tf_op jit(solution)/shard_map/ppermute | solution.py:167
  481.1 5.3 copy-start.5
  481.1 79.0 %all-to-all-start.1 = ((bf16[128,5,2880]{2,1,0:T(8,128)(2,1)}), bf16[128,5,2880]{2,1,0:T(8,128)(2,1)}, u32[]{:S(2)}, u32[]{:S(2)}) async-start(bf16[128,5,2880]{2,1,0:T(8,128)(2,1)} %reshape.329), calls=%async_computation.1 | async-start | bytes 12058624 | tf_op jit(solution)/shard_map/all_to_all | solution.py:169
  583.9 11.0 %copy-start.1 = (bf16[128,2880]{0,1:T(8,128)(2,1)S(1)}, bf16[128,2880]{0,1:T(8,128)(2,1)}, u32[]{:S(2)}) copy-start(bf16[128,2880]{0,1:T(8,128)(2,1)} %param.20) | copy-start | bytes 2211844
Sparse Core Ops, SparseCore 0:
  10.8 101.8 all-gather.2
  115.4 60.2 all-gather.4

commit v2 on v1

--- a/solution.py
+++ b/solution.py
@@ -3,11 +3,130 @@
 import jax
 import jax.numpy as jnp
 from jax import lax
+from jax.experimental import pallas as pl
+from jax.experimental.pallas import tpu as pltpu
 from jax.sharding import PartitionSpec as P
 
 HEADS = 32
 KVH = 8
 HD = 64
+TK = 512
+
+
+def flash_pairs(qpad, qpos, qstart, sink_rows, cache_g, stretch_g, bounds, scale):
+    pairs, rows, lanes = qpad.shape
+    n_cache = cache_g.shape[0] // TK
+    n_blocks = n_cache + stretch_g.shape[0] // TK
+    v_off = cache_g.shape[1] // lanes // 2
+
+    def block_of(j, s):
+        return jnp.minimum(s[0] + j, s[1])
+
+    def kernel(s_ref, q_ref, qpos_ref, qstart_ref, sink_ref, ck_ref, cv_ref, sk_ref, sv_ref, o_ref, m_sc, l_sc, acc_sc):
+        j = pl.program_id(1)
+        b = s_ref[0] + j
+
+        @pl.when(j == 0)
+        def _():
+            m_sc[...] = sink_ref[...]
+            l_sc[...] = jnp.zeros_like(l_sc)
+            acc_sc[...] = jnp.zeros_like(acc_sc)
+
+        def step(k_ref, v_ref):
+            s = lax.dot_general(
+                q_ref[...], k_ref[...], (((1,), (1,)), ((), ())), preferred_element_type=jnp.float32
+            ) * scale
+            kpos = b * TK + lax.broadcasted_iota(jnp.int32, (1, TK), 1)
+            allowed = (kpos <= qpos_ref[...]) & (kpos >= qstart_ref[...])
+            m_prev = m_sc[...]
+            m_new = jnp.maximum(m_prev, jnp.max(jnp.where(allowed, s, -jnp.inf), axis=1, keepdims=True))
+            p = jnp.where(allowed, jnp.exp(s - m_new), 0.0)
+            shrink = jnp.exp(m_prev - m_new)
+            l_sc[...] = l_sc[...] * shrink + jnp.sum(p, axis=1, keepdims=True)
+            acc_sc[...] = acc_sc[...] * shrink + jnp.dot(
+                p.astype(jnp.bfloat16), v_ref[...], preferred_element_type=jnp.float32
+            )
+            m_sc[...] = m_new
+
+        live = b <= s_ref[1]
+
+        @pl.when(live & (b < n_cache))
+        def _():
+            step(ck_ref, cv_ref)
+
+        @pl.when(live & (b >= n_cache))
+        def _():
+            step(sk_ref, sv_ref)
+
+        @pl.when(j == pl.num_programs(1) - 1)
+        def _():
+            denom = l_sc[...] + jnp.exp(sink_ref[...] - m_sc[...])
+            o_ref[...] = (acc_sc[...] / denom).astype(o_ref.dtype)
+
+    def cache_k(p, j, s):
+        return (jnp.minimum(block_of(j, s), n_cache - 1), p)
+
+    def cache_v(p, j, s):
+        return (jnp.minimum(block_of(j, s), n_cache - 1), v_off + p)
+
+    def stretch_k(p, j, s):
+        return (jnp.maximum(block_of(j, s) - n_cache, 0), p)
+
+    def stretch_v(p, j, s):
+        return (jnp.maximum(block_of(j, s) - n_cache, 0), v_off + p)
+
+    grid_spec = pltpu.PrefetchScalarGridSpec(
+        num_scalar_prefetch=1,
+        grid=(pairs, n_blocks),
+        in_specs=[
+            pl.BlockSpec((None, rows, lanes), lambda p, j, s: (p, 0, 0)),
+            pl.BlockSpec((rows, 1), lambda p, j, s: (0, 0)),
+            pl.BlockSpec((rows, 1), lambda p, j, s: (0, 0)),
+            pl.BlockSpec((None, rows, 1), lambda p, j, s: (p, 0, 0)),
+            pl.BlockSpec((TK, lanes), cache_k),
+            pl.BlockSpec((TK, lanes), cache_v),
+            pl.BlockSpec((TK, lanes), stretch_k),
+            pl.BlockSpec((TK, lanes), stretch_v),
+        ],
+        out_specs=pl.BlockSpec((None, rows, lanes), lambda p, j, s: (p, 0, 0)),
+        scratch_shapes=[
+            pltpu.VMEM((rows, 1), jnp.float32),
+            pltpu.VMEM((rows, 1), jnp.float32),
+            pltpu.VMEM((rows, lanes), jnp.float32),
+        ],
+    )
+    flops = 4 * pairs * rows * lanes * TK * n_blocks
+    return pl.pallas_call(
+        kernel,
+        grid_spec=grid_spec,
+        out_shape=jax.ShapeDtypeStruct((pairs, rows, lanes), jnp.bfloat16),
+        compiler_params=pltpu.CompilerParams(dimension_semantics=("arbitrary", "arbitrary")),
+        cost_estimate=pl.CostEstimate(
+            flops=flops // 2,
+            transcendentals=pairs * rows * TK * n_blocks // 2,
+            bytes_accessed=2 * (cache_g.size + stretch_g.size) + 4 * qpad.size,
+        ),
+    )(bounds, qpad, qpos, qstart, sink_rows, cache_g, cache_g, stretch_g, stretch_g)
+
+
+def attention(queries_local, cache_g, stretch_g, sinks, query_pos, query_start):
+    tokens = queries_local.shape[0]
+    groups = HEADS // KVH
+    pairs = KVH // 2
+    q6 = queries_local.reshape(tokens, pairs, 2, groups, HD).transpose(1, 2, 3, 0, 4)
+    zeros = jnp.zeros_like(q6[:, 0])
+    qpad = jnp.stack(
+        [jnp.concatenate([q6[:, 0], zeros], axis=-1), jnp.concatenate([zeros, q6[:, 1]], axis=-1)], axis=1
+    ).reshape(pairs, 2 * groups * tokens, 2 * HD)
+    rows = 2 * groups * tokens
+    qpos = jnp.tile(query_pos, 2 * groups).reshape(rows, 1)
+    qstart = jnp.tile(query_start, 2 * groups).reshape(rows, 1)
+    sink_rows = jnp.repeat(sinks.reshape(pairs, 2 * groups), tokens, axis=1).reshape(pairs, rows, 1)
+    bounds = jnp.stack([query_start[0] // TK, query_pos[-1] // TK]).astype(jnp.int32)
+    out = flash_pairs(qpad, qpos, qstart, sink_rows, cache_g, stretch_g, bounds, 1.0 / math.sqrt(HD))
+    o6 = out.reshape(pairs, 2, groups, tokens, 2, HD)
+    picked = jnp.stack([o6[:, 0, :, :, 0], o6[:, 1, :, :, 1]], axis=1)
+    return picked.transpose(3, 0, 1, 2, 4).reshape(tokens, HEADS * HD)
 
 
 def doc_index(positions, lengths):
@@ -46,67 +165,13 @@
     span = cache_rows + tokens
     query_pos = stretch_base + ctx_here * tokens + jnp.arange(tokens, dtype=jnp.int32)
     lengths = doc_lengths[0]
-    query_doc = doc_index(query_pos, lengths)
-    query_heads = queries[0].reshape(tokens, KVH, groups, HD)
-    sink_grid = sinks.reshape(KVH, groups)
-    local_kv = jnp.concatenate([cache_kv[0], stretch_kv[0]], axis=0)
-    scale = 1.0 / math.sqrt(HD)
-
-    def key_block(carry, keys_values, first):
-        count = keys_values.shape[0]
-        rows = first + jnp.arange(count, dtype=jnp.int32)
-        source = rows // span
-        offset = rows % span
-        key_pos = jnp.where(
-            offset < cache_rows,
-            source * cache_rows + offset,
-            stretch_base + source * tokens + offset - cache_rows,
-        )
-        key_doc = doc_index(key_pos, lengths)
-        allowed = (key_pos[None, :] <= query_pos[:, None]) & (
-            key_doc[None, :] == query_doc[:, None]
-        )
-        keys = keys_values[:, :kv_cols].reshape(count, KVH, HD)
-        values = keys_values[:, kv_cols:].reshape(count, KVH, HD)
-        top, total, numer = carry
-        scores = (
-            jnp.einsum("qkgd,skd->kgqs", query_heads, keys, preferred_element_type=jnp.float32)
-            * scale
-        )
-        masked = jnp.where(allowed[None, None], scores, -jnp.inf)
-        new_top = jnp.maximum(top, jnp.max(masked, axis=-1))
-        weights = jnp.where(allowed[None, None], jnp.exp(scores - new_top[..., None]), 0.0)
-        shrink = jnp.exp(top - new_top)
-        total = total * shrink + jnp.sum(weights, axis=-1)
-        numer = numer * shrink[..., None] + jnp.einsum(
-            "kgqs,skd->kgqd",
-            weights.astype(jnp.bfloat16),
-            values,
-            preferred_element_type=jnp.float32,
-        )
-        return (new_top, total, numer)
-
-    start_top = jnp.broadcast_to(sink_grid[:, :, None], (KVH, groups, tokens))
-    start_total = jnp.zeros((KVH, groups, tokens), jnp.float32)
-    start_numer = jnp.zeros((KVH, groups, tokens, HD), jnp.float32)
-    piece = lax.all_gather(local_kv, "ctx", axis=0, tiled=True)
-    count = piece.shape[0]
-    step_rows = math.gcd(count, 1024)
-
-    def advance(index, state):
-        first = index * step_rows
-        part = lax.dynamic_slice_in_dim(piece, first, step_rows, 0)
-        return key_block(state, part, first)
-
-    top, total, numer = lax.fori_loop(
-        0, count // step_rows, advance, (start_top, start_total, start_numer)
-    )
-    denom = total + jnp.exp(sink_grid[:, :, None] - top)
-    attended = (
-        jnp.transpose(numer / denom[..., None], (2, 0, 1, 3))
-        .reshape(tokens, HEADS * HD)
-        .astype(jnp.bfloat16)
-    )
+    ends = jnp.cumsum(lengths)
+    query_start = jnp.max(
+        jnp.where(ends[None, :] <= query_pos[:, None], ends[None, :], 0), axis=1
+    ).astype(jnp.int32)
+    cache_all = lax.all_gather(cache_kv[0], "ctx", axis=0, tiled=True)
+    stretch_all = lax.all_gather(stretch_kv[0], "ctx", axis=0, tiled=True)
+    attended = attention(queries[0], cache_all, stretch_all, sinks, query_pos, query_start)
     grp_here = lax.axis_index("grp")
     parity = grp_here % 2
     grp_count = lax.axis_size("grp")

time: 613 us -> 544 us (0.89)
  matrix products: 130 us -> 42.1 us
  other arithmetic: 72.8 us -> 15.2 us
  waiting for transfers between devices: 181 us -> 214 us
  Pallas kernels: 0 us -> 27.2 us
  starting transfers between devices: 9.35 us -> 22.4 us
    dot_general x12 -> x0, matrix products: 87.4 us -> none  [the longest x6 44.9 us: key_block(): jnp.einsum('kgqs,skd->kgqd', weights.astype(jnp.bfloat16), values, prefer...]
    reduce_sum x13 -> x0, other arithmetic: 55.5 us -> none  [the longest x6 54.9 us: key_block(): total = total * shrink + jnp.sum(weights, axis=-1)]
    pallas_call x0 -> x1, Pallas kernels: none -> 27.2 us  [flash_pairs(): pl.pallas_call(kernel, grid_spec=grid_spec, out_shape=jax.ShapeDtypeStruc...]
    all_gather x1, waiting for transfers between devices: 0.01 us -> 16.9 us  [body(): lax.all_gather(lax.dynamic_slice_in_dim(out_proj, parity * head_rows, hea...]
    all_gather x1 -> x2, waiting for transfers between devices: 99.8 us -> 116 us  [the longest x1 72.5 us: body(): cache_all = lax.all_gather(cache_kv[0], 'ctx', axis=0, tiled=True)]
    ppermute x1, starting transfers between devices: 1.55 us -> 14.7 us  [body(): partner_cols = lax.ppermute(theirs_cols, 'grp', pair_perm)]
    slice x6 -> x2, local copies, waits for them, and re-layouts: 10.4 us -> 0.81 us  [the longest x1 0.58 us: attention(): query_pos[-1] // TK]
    another operation x2 -> x9, local copies, waits for them, and re-layouts: 0.24 us -> 7.01 us  [the longest x1 3.29 us: attention(): jnp.repeat(sinks.reshape(pairs, 2 * groups), tokens, axis=1)]
  transfers between devices with their start and end apart: 7 -> 8, of which waited for: 5 -> 6; matrix products, arithmetic and copies ran while one was open for 30% -> 6% of each run, Pallas kernels for 0% -> 5%
where the time goes in v2:
time: 544 us; the launch traced here: 533 us
  waiting for transfers between devices  214 us (39%)
  local copies, waits for them, and re-layouts  111 us (20%)
  blocking collectives  84.2 us (15%)
  matrix products  42.1 us (8%)
  Pallas kernels  27.2 us (5%)
  starting transfers between devices  22.4 us (4%)
  between operations  17.3 us (3%)
  other arithmetic  15.2 us (3%)
    all_to_all x1, blocking collectives, body(): lax.all_to_all(split, ('ctx', 'grp'), split_axis=0, concat_axis=0, tiled=...  84.2 us
    all_to_all x1, waiting for transfers between devices, body(): lax.all_to_all(summed.reshape(owners, half_cap, width), ('ctx', 'grp'), s...  73.2 us
    all_gather x1, waiting for transfers between devices, body(): cache_all = lax.all_gather(cache_kv[0], 'ctx', axis=0, tiled=True)  72.5 us
    all_gather x1, waiting for transfers between devices, body(): stretch_all = lax.all_gather(stretch_kv[0], 'ctx', axis=0, tiled=True)  43 us
    pallas_call x1, Pallas kernels, flash_pairs(): pl.pallas_call(kernel, grid_spec=grid_spec, out_shape=jax.ShapeDtypeStruc...  27.2 us
    dot_general x2, matrix products, expert_half(): jnp.dot(rows.reshape(-1, width), in_weights, preferred_element_type=jnp.f...  19.7 us
    all_gather x1, waiting for transfers between devices, body(): lax.all_gather(lax.dynamic_slice_in_dim(out_proj, parity * head_rows, hea...  16.9 us
    dot_general x2, matrix products, expert_half(): jnp.dot(hidden, out_weights, preferred_element_type=jnp.float32)  16.8 us
  transfers between devices with their start and end apart: 8, of which 6 were waited for; matrix products, arithmetic and copies ran while one was open for 6% of the time, Pallas kernels for 5%

profile of v2, /device:TPU:1, one launch (start us, length us, event | category | flops | bytes accessed | tf_op | source)
XLA Modules:
  0.0 533.3 jit_solution(9640342697008865416)
XLA Ops:
  17.9 3.3 reshape_reshape.12.sink_ref
  21.8 43.0 %all-gather.10.cloned.1.call-done = bf16[1,2048,1024]{2,1,0:T(8,128)(2,1)} async-done(((bf16[1,128,1024]{2,1,0:T(8,128)(2,1)}), bf16[1,2048,1024]{2,1,0:T(8,128)(2,1)}) %all-gather.10.cloned.1.call-update) | async-done | bytes 4194320 | tf_op jit(solution)/shard_map/all_gather | solution.py:173
  64.8 72.5 %all-gather.8.cloned.1.call-done = bf16[1,4096,1024]{2,1,0:T(8,128)(2,1)} async-done(((bf16[1,256,1024]{2,1,0:T(8,128)(2,1)}), bf16[1,4096,1024]{2,1,0:T(8,128)(2,1)}) %all-gather.8.cloned.1.call-update) | async-done | bytes 8388624 | tf_op jit(solution)/shard_map/all_gather | solution.py:172
  137.3 27.2 %shard_map.131 = bf16[4,1024,128]{2,1,0:T(8,128)(2,1)} custom-call(s32[2]{0:T(128)} %pad_add_fusion.s_ref, bf16[4,1024,128]{2,1,0:T(8,128)(2,1)} %bitcast.84, s32[1024,1]{1,0:T(8,128)} %copy.64.qpos_ref, s32[1024,1]{1,0:T(8,128)} %copy.65.qstart_ref, f32[4,1024,1]{2,1,0:T(8,128)} %reshape_reshape.12.sink_ref, bf16[4096,1024]{1,0:T(8,128)(2,1)} %bitcast.79, ...), custom_call_target="tpu_custom_call" | custom-call | flops 6442450944 | bytes 14680064 | tf_op jit(solution)/shard_map/pallas_call | solution.py:99
  167.5 14.7 %collective-permute-start = (bf16[128,1024]{0,1:T(8,128)(2,1)S(1)}, bf16[128,1024]{0,1:T(8,128)(2,1)S(1)}, u32[]{:S(2)}, u32[]{:S(2)}) collective-permute-start(bf16[128,1024]{0,1:T(8,128)(2,1)S(1)} %bitcast.88), channel_id=1, source_target_pairs={{0,1},{1,0},{2,3},{3,2},{4,5},{5,4},{6,7},{7,6},{8,9},{9,8},{10,11... | collective-permute-start | bytes 786440 | tf_op jit(solution)/shard_map/ppermute | solution.py:186
  182.3 16.9 %all-gather.6.cloned.1.call-done = bf16[1024,2880]{1,0:T(8,128)(2,1)} async-done(((bf16[64,2880]{1,0:T(8,128)(2,1)}), bf16[1024,2880]{1,0:T(8,128)(2,1)}) %all-gather.6.cloned.1.call-update) | async-done | bytes 5898256 | tf_op jit(solution)/shard_map/all_gather | solution.py:180
  199.2 5.3 fusion.30
  204.5 1.6 copy-done.3
  208.3 1.7 reduce-window.19
  211.1 2.0 fusion.17
  213.9 16.3 %scatter_custom_fusion = bf16[640,2880]{1,0:T(8,128)(2,1)} fusion(s32[512]{0:T(512)S(1)} %bitcast.93, bf16[128,2880]{1,0:T(8,128)(2,1)S(1)} %copy.76, s32[1024]{0:T(1024)S(1)} %pad_clamp_fusion.1, bf16[]{:T(256)} %constant.85.clone.1), kind=kCustom, calls=%fused_computation.13 | custom fusion | bytes 3686402 | tf_op jit(solution)/shard_map/scatter | solution.py:214
  230.1 7.4 %reshape_reshape.11 = bf16[128,5,2880]{2,1,0:T(8,128)(2,1)} reshape(bf16[640,2880]{1,0:T(8,128)(2,1)} %scatter_custom_fusion) | data formatting | bytes 7372800 | tf_op jit(solution)/shard_map/reshape;reshape | solution.py:221
  237.5 84.2 %all_to_all.10 = bf16[128,5,2880]{2,1,0:T(8,128)(2,1)} all-to-all(bf16[128,5,2880]{2,1,0:T(8,128)(2,1)} %reshape_reshape.11), channel_id=1, replica_groups=mesh['ctx'=16,'grp'=8] {'ctx','grp'}, dimensions={0} | all-to-all | bytes 7372800 | tf_op jit(solution)/shard_map/all_to_all | solution.py:222
  321.7 7.9 %copy.77 = bf16[128,5,2880]{0,2,1:T(8,128)(2,1)} copy(bf16[128,5,2880]{2,1,0:T(8,128)(2,1)} %all_to_all.10) | data formatting | bytes 7372800 | tf_op jit(solution)/shard_map/all_to_all | solution.py:222
  330.8 6.4 %collective-permute-done.2 = bf16[128,5,2880]{0,2,1:T(8,128)(2,1)} collective-permute-done((bf16[128,5,2880]{0,2,1:T(8,128)(2,1)}, bf16[128,5,2880]{0,2,1:T(8,128)(2,1)}, u32[]{:S(2)}, u32[]{:S(2)}) %collective-permute-start.2) | collective-permute-done | bytes 3686432 | tf_op jit(solution)/shard_map/ppermute | solution.py:223
  337.2 8.5 %copy.78 = bf16[128,5,2880]{2,1,0:T(8,128)(2,1)} copy(bf16[128,5,2880]{0,2,1:T(8,128)(2,1)} %collective-permute-done.2) | data formatting | bytes 7372800 | tf_op jit(solution)/shard_map/ppermute | solution.py:223
  345.7 8.0 %reshape.198 = bf16[640,2880]{1,0:T(8,128)(2,1)} reshape(bf16[128,5,2880]{2,1,0:T(8,128)(2,1)} %copy.78) | data formatting | bytes 7372800 | tf_op jit(solution)/shard_map/reshape | solution.py:226
  353.7 9.9 %fusion = f32[640,1536]{1,0:T(8,128)S(1)} fusion(bf16[640,2880]{1,0:T(8,128)(2,1)} %reshape.198, bf16[1,2880,1536]{2,1,0:T(8,128)(2,1)} %param.22), kind=kOutput, calls=%fused_computation.3 | convolution fusion | flops 5662310400 | bytes 16465920 | tf_op jit(solution)/shard_map/dot_general | solution.py:226
  363.6 7.9 %convolution_convert_fusion = bf16[640,2880]{0,1:T(8,128)(2,1)} fusion(bf16[1,768,2880]{1,2,0:T(8,128)(2,1)} %param.23, f32[640,1536]{1,0:T(8,128)S(1)} %fusion), kind=kOutput, calls=%fused_computation.9 | convolution fusion | flops 2836930560 | bytes 12042240 | tf_op jit(solution)/shard_map/dot_general | solution.py:228
  371.8 8.2 %reshape.197 = bf16[640,2880]{1,0:T(8,128)(2,1)} reshape(bf16[128,5,2880]{2,1,0:T(8,128)(2,1)} %all_to_all.10) | data formatting | bytes 7372800 | tf_op jit(solution)/shard_map/reshape | solution.py:226
  380.0 9.9 %fusion.2 = f32[640,1536]{1,0:T(8,128)S(1)} fusion(bf16[640,2880]{1,0:T(8,128)(2,1)} %reshape.197, bf16[1,2880,1536]{2,1,0:T(8,128)(2,1)} %param.22), kind=kOutput, calls=%fused_computation.5 | convolution fusion | flops 5662310400 | bytes 16465920 | tf_op jit(solution)/shard_map/dot_general | solution.py:226
  389.9 9.0 %add_convert_fusion = bf16[640,2880]{0,1:T(8,128)(2,1)} fusion(bf16[640,2880]{0,1:T(8,128)(2,1)} %collective-permute-done.3, bf16[1,768,2880]{1,2,0:T(8,128)(2,1)} %param.23, f32[640,1536]{1,0:T(8,128)S(1)} %fusion.2), kind=kOutput, calls=%fused_computation.7 | convolution fusion | flops 2844303360 | bytes 15728640 | tf_op jit(solution)/shard_map/dot_general | solution.py:228
  398.9 6.2 %copy.79 = bf16[640,2880]{1,0:T(8,128)(2,1)} copy(bf16[640,2880]{0,1:T(8,128)(2,1)} %add_convert_fusion) | data formatting | bytes 7372800 | tf_op jit(solution)/shard_map/convert_element_type | solution.py:233
  405.0 7.4 %reshape.199 = bf16[128,5,2880]{2,1,0:T(8,128)(2,1)} reshape(bf16[640,2880]{1,0:T(8,128)(2,1)} %copy.79) | data formatting | bytes 7372800 | tf_op jit(solution)/shard_map/reshape | solution.py:235
  412.4 5.3 all-to-all-start.1
  418.2 73.2 %all-to-all-done.1 = bf16[128,5,2880]{2,1,0:T(8,128)(2,1)} async-done(((bf16[128,5,2880]{2,1,0:T(8,128)(2,1)}), bf16[128,5,2880]{2,1,0:T(8,128)(2,1)}, u32[]{:S(2)}, u32[]{:S(2)}) %all-to-all-start.1) | async-done | bytes 3686432 | tf_op jit(solution)/shard_map/all_to_all | solution.py:234
  491.4 8.0 %reshape.200 = bf16[640,2880]{1,0:T(8,128)(2,1)} reshape(bf16[128,5,2880]{2,1,0:T(8,128)(2,1)} %all-to-all-done.1) | data formatting | bytes 7372800 | tf_op jit(solution)/shard_map/reshape | solution.py:237
  499.3 9.3 %gather_fusion = bf16[512,2880]{1,0:T(8,128)(2,1)} fusion(bf16[640,2880]{1,0:T(8,128)(2,1)} %reshape.200, s32[1024]{0:T(1024)S(1)} %pad_clamp_fusion), kind=kCustom, calls=%fused_computation.1 | custom fusion | bytes 5900288 | tf_op jit(solution)/shard_map/gather | solution.py:238
  508.7 6.5 %reshape.202 = f32[128,4,2880]{2,1,0:T(4,128)} reshape(bf16[512,2880]{1,0:T(8,128)(2,1)} %gather_fusion) | data formatting | bytes 8847360 | tf_op jit(solution)/shard_map/convert_element_type | solution.py:238
  515.2 7.0 %multiply_reduce_fusion = f32[128,2880]{1,0:T(8,128)S(1)} fusion(f32[128,4,2880]{2,1,0:T(4,128)} %reshape.202, f32[128,4]{1,0:T(8,128)S(1)} %copy.80), kind=kLoop, calls=%fused_computation.8 | loop fusion | flops 2580480 | bytes 7374848 | tf_op jit(solution)/shard_map/reduce_sum | solution.py:239
  522.3 1.6 copy.81
  523.8 2.4 fusion.29
  (79 shorter events, 17.5 us)
Async XLA Ops:
  7.2 1.6 copy-start
  7.2 2.9 copy-start.9
  7.2 6.5 %copy-start.4 = (bf16[1,128,2048]{2,1,0:T(8,128)(2,1)S(1)}, bf16[1,128,2048]{2,1,0:T(8,128)(2,1)}, u32[]{:S(2)}) copy-start(bf16[1,128,2048]{2,1,0:T(8,128)(2,1)} %param.13) | copy-start | bytes 1572868
  7.2 57.6 %all-gather.10.cloned.1.call-start = ((), (), s32[]{:S(2)}) async-start(), calls=%async_computation.4 | async-start | bytes 4456448 | tf_op jit(solution)/shard_map/all_gather | solution.py:173
  7.9 129.4 %all-gather.8.cloned.1.call-start = ((), (), s32[]{:S(2)}) async-start(), calls=%async_computation.3 | async-start | bytes 8912896 | tf_op jit(solution)/shard_map/all_gather | solution.py:172
  8.7 190.5 %all-gather.6.cloned.1.call-start = ((), (), s32[]{:S(2)}) async-start(), calls=%async_computation.2 | async-start | bytes 6406144 | tf_op jit(solution)/shard_map/all_gather | solution.py:180
  14.0 3.7 copy-start.8
  167.5 31.6 %collective-permute-start = (bf16[128,1024]{0,1:T(8,128)(2,1)S(1)}, bf16[128,1024]{0,1:T(8,128)(2,1)S(1)}, u32[]{:S(2)}, u32[]{:S(2)}) collective-permute-start(bf16[128,1024]{0,1:T(8,128)(2,1)S(1)} %bitcast.88), channel_id=1, source_target_pairs={{0,1},{1,0},{2,3},{3,2},{4,5},{5,4},{6,7},{7,6},{8,9},{9,8},{10,11... | collective-permute-start | bytes 786440 | tf_op jit(solution)/shard_map/ppermute | solution.py:186
  199.2 8.8 %copy-start.6 = (s32[1,128,4]{1,2,0:T(4,128)S(1)}, s32[1,128,4]{1,2,0:T(4,128)}, u32[]{:S(2)}) copy-start(s32[1,128,4]{1,2,0:T(4,128)} %param.21) | copy-start | bytes 6148
  204.5 1.6 copy-start.3
  206.1 7.0 %copy-start.7 = (f32[2880]{0:T(1024)S(1)}, f32[2880]{0:T(1024)}, u32[]{:S(2)}) copy-start(f32[2880]{0:T(1024)} %param.19) | copy-start | bytes 34564
  207.3 3.8 collective-permute-start.1
  213.0 310.8 %copy-start.2 = (bf16[128,2880]{0,1:T(8,128)(2,1)}, bf16[128,2880]{0,1:T(8,128)(2,1)S(1)}, u32[]{:S(2)}) copy-start(bf16[128,2880]{0,1:T(8,128)(2,1)S(1)} %get-tuple-element.3) | copy-start | bytes 2211844
  329.6 7.7 %collective-permute-start.2 = (bf16[128,5,2880]{0,2,1:T(8,128)(2,1)}, bf16[128,5,2880]{0,2,1:T(8,128)(2,1)}, u32[]{:S(2)}, u32[]{:S(2)}) collective-permute-start(bf16[128,5,2880]{0,2,1:T(8,128)(2,1)} %copy.77), channel_id=1, source_target_pairs={{0,1},{1,0},{2,3},{3,2},{4,5},{5,4},{6,7},{7,6},{8,9},{9,8},{10,11... | collective-permute-start | bytes 11059208 | tf_op jit(solution)/shard_map/ppermute | solution.py:223
  371.4 18.4 %collective-permute-start.3 = (bf16[640,2880]{0,1:T(8,128)(2,1)}, bf16[640,2880]{0,1:T(8,128)(2,1)}, u32[]{:S(2)}, u32[]{:S(2)}) collective-permute-start(bf16[640,2880]{0,1:T(8,128)(2,1)} %convolution_convert_fusion), channel_id=1, source_target_pairs={{0,1},{1,0},{2,3},{3,2},{4,5},{5,4},{6,7},{7,6},{8,9},{9,8},{10,11... | collective-permute-start | bytes 11059208 | tf_op jit(solution)/shard_map/ppermute | solution.py:232
  412.4 5.3 copy-start.5
  412.4 79.0 %all-to-all-start.1 = ((bf16[128,5,2880]{2,1,0:T(8,128)(2,1)}), bf16[128,5,2880]{2,1,0:T(8,128)(2,1)}, u32[]{:S(2)}, u32[]{:S(2)}) async-start(bf16[128,5,2880]{2,1,0:T(8,128)(2,1)} %reshape.199), calls=%async_computation.1 | async-start | bytes 12058624 | tf_op jit(solution)/shard_map/all_to_all | solution.py:234
  515.2 11.0 %copy-start.1 = (bf16[128,2880]{0,1:T(8,128)(2,1)S(1)}, bf16[128,2880]{0,1:T(8,128)(2,1)}, u32[]{:S(2)}) copy-start(bf16[128,2880]{0,1:T(8,128)(2,1)} %param.18) | copy-start | bytes 2211844
Sparse Core Ops, SparseCore 0:
  10.2 54.5 all-gather.9
  67.0 70.3 all-gather.7
  139.5 59.6 all-gather.5
